TPU v7x, 256 devices: a whole 4x4x8 slice. The times are simulated.
256 devices in a mesh: dp: 4 (over y), seq: 64 (over z, x, core).
Axes of the slice: x: 4, y: 4, z: 8, core: 2. Of those that a mesh axis runs over, the one named last changes fastest.
Arguments:
- features: bfloat16 [49152, 1408], P(('dp', 'seq')), parts along dimension 0, may hold values from -6 to 6
- norm_gain: float32 [1408], replicated, may hold values from 0.1 to 1.9
- conv_weight: bfloat16 [5, 1408, 1536], P(None, None, 'seq'), may hold values from -0.0625 to 0.0625
- conv_bias: float32 [1536], replicated, may hold values from -3 to 3
- attn_gain: float32 [1536], replicated, may hold values from 0.1 to 1.9
- query_weight: bfloat16 [1536, 1024], P('seq'), may hold values from -1 to 1
- keyval_weight: bfloat16 [1536, 256], P('seq'), may hold values from -1 to 1
- head_scale: float32 [8], replicated, may hold values from 1 to 4
- output_weight: bfloat16 [1024, 1536], P('seq'), may hold values from -0.1875 to 0.1875
Outputs:
- coarse: bfloat16 [24576, 1536], P(('dp', 'seq')), parts along dimension 0
- attended: bfloat16 [24576, 1536], P(('dp', 'seq')), parts along dimension 0
There are 4 independent parts, one for each index of `dp`. A program takes and returns all parts, laid end to end along the dimension named above; an argument that names none is the same for every part. Nothing has to cross between parts.
All inputs are finite; a program needn't handle non-finite values.
Results may differ from a plain program's by a relative error of at most 0.007.
Values may be sent and summed in bfloat16 or wider, within the bound.
No kernel may reach another device: no remote copies, remote signals or barrier semaphores. Data moves between devices by JAX's collectives and lax.ppermute only.
A program may use at most 128 MiB of HBM per device.

v0:
```python
import jax
import jax.numpy as jnp
from jax import lax
from jax.sharding import Mesh
from jax.sharding import PartitionSpec as P

HEAD_DIM = 128


def normalize(values_in, channel_gain):
    meansq = jnp.mean(values_in * values_in, axis=-1, keepdims=True)
    return values_in * lax.rsqrt(meansq + 1e-06) * channel_gain


def convolve(padded, kernel, row_count):
    summed = jnp.zeros((row_count, kernel.shape[2]), jnp.float32)
    for kernel_tap in range(kernel.shape[0]):
        summed = summed + jnp.dot(
            padded[kernel_tap : kernel_tap + row_count],
            kernel[kernel_tap],
            preferred_element_type=jnp.float32,
        )
    return summed


def pool_pairs(levels):
    return jnp.max(levels.reshape(-1, 2, levels.shape[1]), axis=1)


def spread_in_plane(block):
    inner = lax.all_gather(block, "sxx", axis=0, tiled=True)
    return lax.all_gather(inner, "core", axis=0, tiled=True)


def plane_order(columns, nz, nxx, nc):
    rows = columns.shape[0]
    return (
        columns.reshape(rows, nz, nxx, nc, -1)
        .transpose(0, 3, 2, 1, 4)
        .reshape(rows, columns.shape[1])
    )


def attend(queries, key_block, scales):
    row_count = queries.shape[0]
    head_count = scales.shape[0]
    shaped = queries.reshape(row_count, head_count, HEAD_DIM)
    key_part = key_block[:, :HEAD_DIM]
    value_part = key_block[:, HEAD_DIM:]
    scores = (
        jnp.einsum("qhd,kd->hqk", shaped, key_part, preferred_element_type=jnp.float32)
        * scales[:, None, None]
        * HEAD_DIM ** (-0.5)
    )
    biggest = jnp.max(scores, axis=2)
    expon = jnp.exp(scores - biggest[:, :, None])
    total = jnp.sum(expon, axis=2)
    context = jnp.einsum(
        "hqk,kd->hqd", expon.astype(jnp.bfloat16), value_part, preferred_element_type=jnp.float32
    )
    context = context / total[:, :, None]
    return context.transpose(1, 0, 2).reshape(row_count, head_count * HEAD_DIM).astype(jnp.bfloat16)


def shards(
    features,
    norm_gain,
    conv_weight,
    conv_bias,
    attn_gain,
    query_weight,
    keyval_weight,
    head_scale,
    output_weight,
):
    nz = lax.axis_size("sz")
    nxx = lax.axis_size("sxx")
    nc = lax.axis_size("core")
    nx = nxx * nc
    me_x = lax.axis_index("sxx") * nc + lax.axis_index("core")
    rows_here = features.shape[0]
    taps, ch_in, width = conv_weight.shape
    ch_out = conv_bias.shape[0]
    proj_piece = jnp.concatenate([query_weight, keyval_weight], axis=1)
    pieces = [conv_weight, proj_piece, output_weight]
    sizes = [p.size for p in pieces]
    flat = jnp.concatenate([p.reshape(-1) for p in pieces])
    got = lax.all_gather(flat, "sz", axis=0, tiled=False)
    kernel = (
        got[:, : sizes[0]]
        .reshape(nz, taps, ch_in, width)
        .transpose(1, 2, 0, 3)
        .reshape(taps, ch_in, nz * width)
    )
    proj_z = got[:, sizes[0] : sizes[0] + sizes[1]].reshape(
        nz * proj_piece.shape[0], proj_piece.shape[1]
    )
    out_z = got[:, sizes[0] + sizes[1] :].reshape(
        nz * output_weight.shape[0], output_weight.shape[1]
    )
    normed = jax.nn.gelu(normalize(features.astype(jnp.float32), norm_gain)).astype(jnp.bfloat16)
    plane = lax.all_gather(normed, ("sxx", "core"), axis=0, tiled=True)
    plane_rows = plane.shape[0]
    forward = [(i, i + 1) for i in range(nz - 1)]
    backward = [(i + 1, i) for i in range(nz - 1)]
    low = lax.ppermute(plane[plane_rows - 2 :], "sz", forward)
    high = lax.ppermute(plane[:2], "sz", backward)
    padded = jnp.concatenate([low, plane, high], axis=0)
    bias_all = conv_bias.reshape(nz, nx, width).transpose(1, 0, 2)
    bias = lax.dynamic_index_in_dim(bias_all, me_x, axis=0, keepdims=False).reshape(nz * width)
    levels = convolve(padded, kernel, plane_rows) + bias[None, :]
    pooled = pool_pairs(levels).astype(jnp.bfloat16)
    proj_weight = spread_in_plane(proj_z)
    coarse_rows = rows_here // 2
    parts = pooled.reshape(nx, coarse_rows, nz * width)
    received = lax.all_to_all(parts, ("sxx", "core"), 0, 0, tiled=False)
    coarse = (
        received.reshape(nx, coarse_rows, nz, width)
        .transpose(1, 2, 0, 3)
        .reshape(coarse_rows, ch_out)
    )
    attn_in = normalize(coarse.astype(jnp.float32), attn_gain).astype(jnp.bfloat16)
    proj = jnp.dot(
        plane_order(attn_in, nz, nxx, nc), proj_weight, preferred_element_type=jnp.float32
    )
    q_cols = query_weight.shape[1]
    queries = proj[:, :q_cols].astype(jnp.bfloat16)
    keyvals = proj[:, q_cols:].astype(jnp.bfloat16)
    key_block = spread_in_plane(lax.all_gather(keyvals, "sz", axis=0, tiled=True))
    out_weight = spread_in_plane(out_z)
    context = attend(queries, key_block, head_scale)
    projected = jnp.dot(
        plane_order(context, nz, nxx, nc), out_weight, preferred_element_type=jnp.float32
    )
    return (coarse, projected.astype(jnp.bfloat16))


def solution(mesh):
    dp = mesh.shape["dp"]
    seq = mesh.shape["seq"]
    nc = 2 if seq % 2 == 0 else 1
    nxx = 4 if seq // nc % 4 == 0 else seq // nc
    nz = seq // (nc * nxx)
    grid = Mesh(mesh.devices.reshape(dp, nz, nxx, nc), ("dp", "sz", "sxx", "core"))
    seq_axes = ("sz", "sxx", "core")
    rows = P(("dp",) + seq_axes, None)
    return jax.shard_map(
        shards,
        mesh=grid,
        in_specs=(
            rows,
            P(),
            P(None, None, seq_axes),
            P(),
            P(),
            P(seq_axes, None),
            P(seq_axes, None),
            P(),
            P(seq_axes, None),
        ),
        out_specs=(rows, rows),
        check_vma=False,
    )
```

profile of v0, /device:TPU:1, one launch (start us, length us, event | category | flops | bytes accessed | tf_op | source)
XLA Modules:
  0.0 313.2 jit_solution(10841448251101722798)
XLA Ops:
  7.3 2.1 copy.56
  9.4 2.4 reshape.100
  14.5 51.2 %all-gather.24.cloned.1.call-done = bf16[1794048]{0:T(1024)(128)(2,1)} async-done(((bf16[224256]{0:T(1024)(128)(2,1)}), bf16[1794048]{0:T(1024)(128)(2,1)}) %all-gather.24.cloned.1.call-update) | async-done | bytes 3588112 | tf_op jit(solution)/shard_map/all_gather | solution.py:88
  65.7 5.4 %reshape.114 = bf16[8,224256]{1,0:T(8,128)(2,1)} reshape(bf16[1794048]{0:T(1024)(128)(2,1)} %all-gather.24.cloned.1.call-done) | data formatting | bytes 7176192 | tf_op jit(solution)/shard_map/all_gather | solution.py:88
  73.6 2.8 reshape.124
  76.4 22.4 %reshape.103 = bf16[8,5,1408,24]{3,2,1,0:T(8,128)(2,1)} reshape(bf16[1351680]{0:T(1024)(128)(2,1)} %reshape.124) | data formatting | bytes 5406720 | tf_op jit(solution)/shard_map/reshape | solution.py:91
  98.8 10.0 %fusion.56 = (bf16[1,1408,8,24]{3,1,0,2:T(8,128)(2,1)S(1)}, bf16[1,1408,8,24]{3,1,0,2:T(8,128)(2,1)}, bf16[1,1408,8,24]{3,1,0,2:T(8,128)(2,1)}, bf16[1,1408,8,24]{3,1,0,2:T(8,128)(2,1)}, bf16[1,1408,8,24]{3,1,0,2:T(8,128)(2,1)}) fusion(bf16[5,1408,8,24]{3,1,0,2:T(8,128)(2,1)} %bitcast.78), kind=kLoop, calls=%fused_computation.61 | loop fusion | bytes 5406720 | tf_op jit(solution)/shard_map/slice | solution.py:20
  108.8 3.7 %copy.58 = bf16[1,1408,8,24]{1,3,2,0:T(8,128)(2,1)} copy(bf16[1,1408,8,24]{3,1,0,2:T(8,128)(2,1)} %get-tuple-element.13) | data formatting | bytes 1081344 | tf_op jit(solution)/shard_map/slice | solution.py:20
  112.5 3.8 %copy.59 = bf16[1,1408,8,24]{1,3,2,0:T(8,128)(2,1)} copy(bf16[1,1408,8,24]{3,1,0,2:T(8,128)(2,1)} %get-tuple-element.12) | data formatting | bytes 1081344 | tf_op jit(solution)/shard_map/slice | solution.py:20
  116.4 3.8 %copy.57 = bf16[1,1408,8,24]{1,3,2,0:T(8,128)(2,1)} copy(bf16[1,1408,8,24]{3,1,0,2:T(8,128)(2,1)} %get-tuple-element.14) | data formatting | bytes 1081344 | tf_op jit(solution)/shard_map/slice | solution.py:20
  120.2 3.8 %copy.61 = bf16[1,1408,8,24]{1,3,2,0:T(8,128)(2,1)} copy(bf16[1,1408,8,24]{3,1,0,2:T(8,128)(2,1)} %get-tuple-element.11) | data formatting | bytes 1081344 | tf_op jit(solution)/shard_map/slice | solution.py:20
  124.0 1.7 copy.60
  127.8 1.5 collective-permute-start.1
  129.3 6.1 %all-gather.12.cloned.1.call-done = bf16[768,1280]{1,0:T(8,128)(2,1)} async-done(((bf16[192,1280]{1,0:T(8,128)(2,1)}), bf16[768,1280]{1,0:T(8,128)(2,1)}) %all-gather.12.cloned.1.call-update) | async-done | bytes 1966096 | tf_op jit(solution)/shard_map/all_gather | solution.py:31
  135.4 2.7 constant_dynamic-update-slice_fusion.1
  139.1 1.6 fusion.58
  140.7 1.6 fusion.12
  142.3 1.6 fusion.8
  143.9 1.6 fusion.26
  145.6 1.7 fusion.20
  147.9 2.2 reduce_max.18
  151.6 4.2 %all-to-all-start = ((bf16[8,96,192]{1,2,0:T(8,128)(2,1)}), bf16[8,96,192]{1,2,0:T(8,128)(2,1)S(1)}, u32[]{:S(2)}, u32[]{:S(2)}) async-start(bf16[8,96,192]{1,2,0:T(8,128)(2,1)} %copy.64), calls=%async_computation | async-start | bytes 786432 | tf_op jit(solution)/shard_map/all_to_all | solution.py:116
  155.9 7.6 %all-to-all-done = bf16[8,96,192]{1,2,0:T(8,128)(2,1)S(1)} async-done(((bf16[8,96,192]{1,2,0:T(8,128)(2,1)}), bf16[8,96,192]{1,2,0:T(8,128)(2,1)S(1)}, u32[]{:S(2)}, u32[]{:S(2)}) %all-to-all-start) | async-done | bytes 294944 | tf_op jit(solution)/shard_map/all_to_all | solution.py:116
  164.1 2.8 convolution_convert_fusion.1
  166.9 22.5 %all_gather.35 = bf16[768,256]{1,0:T(8,128)(2,1)} all-gather(bf16[96,256]{1,0:T(8,128)(2,1)S(1)} %slice.96), channel_id=1, replica_groups=mesh['dp'=4,'sz'=8,'sxx'=4,'core'=2] {'sz'}, dimensions={0}, use_global_device_ids=true | all-gather | bytes 442368 | tf_op jit(solution)/shard_map/all_gather | solution.py:129
  190.5 32.7 %all-gather.16.cloned.1.call-done = bf16[3072,256]{1,0:T(8,128)(2,1)} async-done(((bf16[768,256]{1,0:T(8,128)(2,1)}), bf16[3072,256]{1,0:T(8,128)(2,1)}) %all-gather.16.cloned.1.call-update) | async-done | bytes 1572880 | tf_op jit(solution)/shard_map/all_gather | solution.py:31
  224.4 29.5 %all-gather.20.cloned.1.call-done = bf16[512,1536]{1,0:T(8,128)(2,1)} async-done(((bf16[128,1536]{1,0:T(8,128)(2,1)}), bf16[512,1536]{1,0:T(8,128)(2,1)}) %all-gather.20.cloned.1.call-update) | async-done | bytes 1572880 | tf_op jit(solution)/shard_map/all_gather | solution.py:31
  253.9 20.2 %all-gather.18.cloned.1.call-done = bf16[6144,256]{1,0:T(8,128)(2,1)} async-done(((bf16[3072,256]{1,0:T(8,128)(2,1)}), bf16[6144,256]{1,0:T(8,128)(2,1)}) %all-gather.18.cloned.1.call-update) | async-done | bytes 3145744 | tf_op jit(solution)/shard_map/all_gather | solution.py:32
  274.1 9.2 %bitcast_reduce_fusion = (f32[8,96]{1,0:T(8,128)S(1)}, f32[6144,96,8]{0,1,2:T(8,128)}) fusion(f32[8]{0:T(128)S(1)} %copy-done.8, bf16[6144,256]{1,0:T(8,128)(2,1)} %all-gather.18.cloned.1.call-done, bf16[96,1280]{1,0:T(8,128)(2,1)S(1)} %convolution_convert_fusion.1), kind=kOutput, calls=%fused_computation.1 | convolution fusion | flops 1222114560 | bytes 20647424 | tf_op jit(solution)/shard_map/qhd,kd->hqk/dot_general | solution.py:51
  283.3 11.1 %fusion.1 = f32[8,96]{1,0:T(8,128)S(1)} fusion(f32[6144,96,8]{0,1,2:T(8,128)} %get-tuple-element.18, f32[8,96]{1,0:T(8,128)S(1)} %get-tuple-element.17, f32[8]{0:T(128)S(1)} %copy-done.8), kind=kLoop, calls=%fused_computation.4 | loop fusion | flops 18873600 | bytes 18880544 | tf_op jit(solution)/shard_map/reduce_sum | solution.py:57
  294.4 8.4 %fusion.46 = bf16[96,8,128]{2,0,1:T(8,128)(2,1)S(1)} fusion(bf16[6144,256]{1,0:T(8,128)(2,1)S(1)} %copy-done.1, f32[6144,96,8]{0,1,2:T(8,128)} %get-tuple-element.18, f32[8,96]{1,0:T(8,128)S(1)} %get-tuple-element.17, f32[8]{0:T(128)S(1)} %copy-done.8, f32[96,8]{0,1:T(8,128)S(1)} %bitcast.93), kind=kOutput, calls=%fused_computation.43 | convolution fusion | flops 1227030528 | bytes 20652544 | tf_op jit(solution)/shard_map/hqk,kd->hqd/dot_general | solution.py:58
  303.1 3.3 %convolution_convert_fusion = bf16[96,1536]{1,0:T(8,128)(2,1)} fusion(bf16[96,1024]{0,1:T(8,128)(2,1)S(1)} %bitcast.86, bf16[1024,1536]{1,0:T(8,128)(2,1)} %all-gather.22.cloned.1.call-done), kind=kOutput, calls=%fused_computation.23 | convolution fusion | flops 302137344 | bytes 3637248 | tf_op jit(solution)/shard_map/dot_general | solution.py:132
  (87 shorter events, 13.5 us)
Async XLA Ops:
  7.2 4.6 %copy-start.7 = (bf16[24,1024]{1,0:T(8,128)(2,1)S(1)}, bf16[24,1024]{1,0:T(8,128)(2,1)}, u32[]{:S(2)}) copy-start(bf16[24,1024]{1,0:T(8,128)(2,1)} %param.14) | copy-start | bytes 147460
  7.2 4.6 %copy-start.9 = (bf16[24,256]{1,0:T(8,128)(2,1)S(1)}, bf16[24,256]{1,0:T(8,128)(2,1)}, u32[]{:S(2)}) copy-start(bf16[24,256]{1,0:T(8,128)(2,1)} %param.15) | copy-start | bytes 36868
  7.2 4.8 %copy-start.6 = (bf16[16,1536]{1,0:T(8,128)(2,1)S(1)}, bf16[16,1536]{1,0:T(8,128)(2,1)}, u32[]{:S(2)}) copy-start(bf16[16,1536]{1,0:T(8,128)(2,1)} %param.17) | copy-start | bytes 147460
  7.2 5.7 %copy-start = (bf16[192,1408]{1,0:T(8,128)(2,1)S(1)}, bf16[192,1408]{1,0:T(8,128)(2,1)}, u32[]{:S(2)}) copy-start(bf16[192,1408]{1,0:T(8,128)(2,1)} %param.9) | copy-start | bytes 1622020
  7.2 5.9 %copy-start.10 = (f32[1408]{0:T(1024)S(1)}, f32[1408]{0:T(1024)}, u32[]{:S(2)}) copy-start(f32[1408]{0:T(1024)} %param.10) | copy-start | bytes 16900
  7.2 58.5 %all-gather.24.cloned.1.call-start = ((), (), s32[]{:S(2)}) async-start(), calls=%async_computation.8 | async-start | bytes 4036608 | tf_op jit(solution)/shard_map/all_gather | solution.py:88
  12.9 112.8 %all-gather.10.cloned.1.call-start = ((), (), s32[]{:S(2)}) async-start(), calls=%async_computation.1 | async-start | bytes 4866048 | tf_op jit(solution)/shard_map/all_gather | solution.py:102
  14.5 59.0 %copy-start.11 = (f32[1536]{0:T(1024)S(1)}, f32[1536]{0:T(1024)}, u32[]{:S(2)}) copy-start(f32[1536]{0:T(1024)} %param.12) | copy-start | bytes 18436
  14.5 120.9 %all-gather.12.cloned.1.call-start = ((), (), s32[]{:S(2)}) async-start(), calls=%async_computation.2 | async-start | bytes 2457600 | tf_op jit(solution)/shard_map/all_gather | solution.py:31
  71.1 2.6 slice-start
  73.4 90.7 %all-gather.14.cloned.1.call-start = ((), (), s32[]{:S(2)}) async-start(), calls=%async_computation.3 | async-start | bytes 5898240 | tf_op jit(solution)/shard_map/all_gather | solution.py:32
  126.5 14.2 %collective-permute-start = (bf16[2,1408]{1,0:T(2,128)(2,1)S(1)}, bf16[2,1408]{1,0:T(2,128)(2,1)S(1)}, u32[]{:S(2)}, u32[]{:S(2)}) collective-permute-start(bf16[2,1408]{1,0:T(2,128)(2,1)S(1)} %get-tuple-element.15), channel_id=1, source_target_pairs={{0,8},{8,16},{16,24},{24,32},{32,40},{40,48},{48,56},{1,9},{9,17},... | collective-permute-start | bytes 16904 | tf_op jit(solution)/shard_map/ppermute | solution.py:106
  127.8 12.8 %collective-permute-start.1 = (bf16[2,1408]{1,0:T(2,128)(2,1)S(1)}, bf16[2,1408]{1,0:T(2,128)(2,1)S(1)}, u32[]{:S(2)}, u32[]{:S(2)}) collective-permute-start(bf16[2,1408]{1,0:T(2,128)(2,1)S(1)} %get-tuple-element.16), channel_id=1, source_target_pairs={{8,0},{16,8},{24,16},{32,24},{40,32},{48,40},{56,48},{9,1},{17,9},... | collective-permute-start | bytes 16904 | tf_op jit(solution)/shard_map/ppermute | solution.py:107
  135.4 2.8 slice-start.2
  135.4 3.5 %slice-start.3 = ((s8[4325376]{0:T(1024)(128)(4,1)}), s8[4194304]{0:T(1024)(128)(4,1)S(1)}, s32[]{:S(2)}) async-start(s8[4325376]{0:T(1024)(128)(4,1)} %bitcast.82), calls=%async_computation.12 | async-start | bytes 8388608
  135.4 3.6 %copy-start.5 = (bf16[1,1408,8,24]{1,3,2,0:T(8,128)(2,1)S(1)}, bf16[1,1408,8,24]{1,3,2,0:T(8,128)(2,1)}, u32[]{:S(2)}) copy-start(bf16[1,1408,8,24]{1,3,2,0:T(8,128)(2,1)} %copy.59) | copy-start | bytes 1622020
  138.1 2.6 copy-start.3
  140.7 1.6 copy-start.4
  142.3 1.6 copy-start.2
  147.3 8.5 %copy-start.12 = (f32[1536]{0:T(1024)S(1)}, f32[1536]{0:T(1024)}, u32[]{:S(2)}) copy-start(f32[1536]{0:T(1024)} %param.13) | copy-start | bytes 18436
  151.6 11.9 %all-to-all-start = ((bf16[8,96,192]{1,2,0:T(8,128)(2,1)}), bf16[8,96,192]{1,2,0:T(8,128)(2,1)S(1)}, u32[]{:S(2)}, u32[]{:S(2)}) async-start(bf16[8,96,192]{1,2,0:T(8,128)(2,1)} %copy.64), calls=%async_computation | async-start | bytes 786432 | tf_op jit(solution)/shard_map/all_to_all | solution.py:116
  155.8 33.7 %slice-start.1 = ((bf16[8,224256]{1,0:T(8,128)(2,1)}), bf16[8,24576]{1,0:T(8,128)(2,1)S(1)}, s32[]{:S(2)}) async-start(bf16[8,224256]{1,0:T(8,128)(2,1)} %reshape.114), calls=%async_computation.10 | async-start | bytes 786432 | tf_op jit(solution)/shard_map/slice | solution.py:98
  155.8 67.4 %all-gather.16.cloned.1.call-start = ((), (), s32[]{:S(2)}) async-start(), calls=%async_computation.4 | async-start | bytes 1966080 | tf_op jit(solution)/shard_map/all_gather | solution.py:31
  166.9 107.2 %copy-start.8 = (f32[8]{0:T(128)S(1)}, f32[8]{0:T(128)}, u32[]{:S(2)}) copy-start(f32[8]{0:T(128)} %param.16) | copy-start | bytes 100
  189.4 64.4 %all-gather.20.cloned.1.call-start = ((), (), s32[]{:S(2)}) async-start(), calls=%async_computation.6 | async-start | bytes 1966080 | tf_op jit(solution)/shard_map/all_gather | solution.py:31
  190.4 83.6 %all-gather.18.cloned.1.call-start = ((), (), s32[]{:S(2)}) async-start(), calls=%async_computation.5 | async-start | bytes 4718592 | tf_op jit(solution)/shard_map/all_gather | solution.py:32
  223.2 79.9 %all-gather.22.cloned.1.call-start = ((), (), s32[]{:S(2)}) async-start(), calls=%async_computation.7 | async-start | bytes 4718592 | tf_op jit(solution)/shard_map/all_gather | solution.py:32
  283.3 11.1 %copy-start.1 = (bf16[6144,256]{1,0:T(8,128)(2,1)S(1)}, bf16[6144,256]{1,0:T(8,128)(2,1)}, u32[]{:S(2)}) copy-start(bf16[6144,256]{1,0:T(8,128)(2,1)} %all-gather.18.cloned.1.call-done) | copy-start | bytes 9437188
Sparse Core Ops, SparseCore 0:
  13.0 52.6 all-gather.23
  67.6 34.2 all-gather.9
  103.7 31.6 all-gather.11
  137.0 19.5 all-gather.13
  189.6 33.5 all-gather.15
  224.8 28.9 all-gather.19
  255.7 18.3 all-gather.17
  275.8 18.7 all-gather.21
where the time goes:
time: 314 us; the launch traced here: 313 us
  waiting for transfers between devices  147 us (47%)
  local copies, waits for them, and re-layouts  73.3 us (23%)
  matrix products  31.8 us (10%)
  blocking collectives  22.5 us (7%)
  other arithmetic  16.2 us (5%)
  between operations  14.6 us (5%)
  starting transfers between devices  7.52 us (2%)
    all_gather x3, waiting for transfers between devices, spread_in_plane(): inner = lax.all_gather(block, 'sxx', axis=0, tiled=True)  68.2 us
    all_gather x1, waiting for transfers between devices, shards(): got = lax.all_gather(flat, 'sz', axis=0, tiled=False)  51.2 us
    slice x6, local copies, waits for them, and re-layouts, convolve(): kernel[kernel_tap]  26.8 us
    all_gather x1, blocking collectives, shards(): lax.all_gather(keyvals, 'sz', axis=0, tiled=True)  22.5 us
    reshape x1, local copies, waits for them, and re-layouts, shards(): kernel = got[:, :sizes[0]].reshape(nz, taps, ch_in, width).transpose(1, 2...  22.4 us
    all_gather x3, waiting for transfers between devices, spread_in_plane(): return lax.all_gather(inner, 'core', axis=0, tiled=True)  20.2 us
    reduce_sum x1, other arithmetic, attend(): total = jnp.sum(expon, axis=2)  11.1 us
    unnamed x34, local copies, waits for them, and re-layouts  9.51 us
  transfers between devices with their start and end apart: 11, of which 6 were waited for; matrix products, arithmetic and copies ran while one was open for 35% of the time, Pallas kernels for 0%

commit v1 on v0

--- a/solution.py
+++ b/solution.py
@@ -1,10 +1,21 @@
+import functools
 import jax
 import jax.numpy as jnp
 from jax import lax
 from jax.sharding import Mesh
 from jax.sharding import PartitionSpec as P
+from jax.lax import all_to_all, axis_size
 
 HEAD_DIM = 128
+
+
+def try_all_the_matrix(x_part, row_axis):
+    return jnp.concatenate(
+        all_to_all(jnp.stack(axis_size(row_axis) * [x_part]), row_axis, 0, 0), axis=0
+    )
+
+
+begin_samples = functools.partial(try_all_the_matrix, row_axis="sz")
 
 
 def normalize(values_in, channel_gain):
@@ -126,7 +137,7 @@
     q_cols = query_weight.shape[1]
     queries = proj[:, :q_cols].astype(jnp.bfloat16)
     keyvals = proj[:, q_cols:].astype(jnp.bfloat16)
-    key_block = spread_in_plane(lax.all_gather(keyvals, "sz", axis=0, tiled=True))
+    key_block = spread_in_plane(begin_samples(keyvals))
     out_weight = spread_in_plane(out_z)
     context = attend(queries, key_block, head_scale)
     projected = jnp.dot(

time: 314 us -> 303 us (0.965)
  waiting for transfers between devices: 147 us -> 138 us
    all_gather x1 -> x0, blocking collectives: 22.5 us -> none  [shards(): lax.all_gather(keyvals, 'sz', axis=0, tiled=True)]
    all_to_all x0 -> x1, blocking collectives: none -> 20 us  [try_all_the_matrix(): all_to_all(jnp.stack(axis_size(row_axis) * [x_part]), row_axis, 0, 0)]
    all_gather x3, waiting for transfers between devices: 68.2 us -> 59.4 us  [spread_in_plane(): inner = lax.all_gather(block, 'sxx', axis=0, tiled=True)]
  transfers between devices with their start and end apart: 11 -> 11, of which waited for: 6 -> 6; matrix products, arithmetic and copies ran while one was open for 35% -> 36% of each run, Pallas kernels for 0% -> 0%
where the time goes in v1:
time: 303 us; the launch traced here: 302 us
  waiting for transfers between devices  138 us (46%)
  local copies, waits for them, and re-layouts  73.3 us (24%)
  matrix products  31.8 us (10%)
  blocking collectives  20 us (7%)
  other arithmetic  16.2 us (5%)
  between operations  14.6 us (5%)
  starting transfers between devices  7.52 us (2%)
    all_gather x3, waiting for transfers between devices, spread_in_plane(): inner = lax.all_gather(block, 'sxx', axis=0, tiled=True)  59.4 us
    all_gather x1, waiting for transfers between devices, shards(): got = lax.all_gather(flat, 'sz', axis=0, tiled=False)  51.2 us
    slice x6, local copies, waits for them, and re-layouts, convolve(): kernel[kernel_tap]  26.8 us
    reshape x1, local copies, waits for them, and re-layouts, shards(): kernel = got[:, :sizes[0]].reshape(nz, taps, ch_in, width).transpose(1, 2...  22.4 us
    all_gather x3, waiting for transfers between devices, spread_in_plane(): return lax.all_gather(inner, 'core', axis=0, tiled=True)  20.2 us
    all_to_all x1, blocking collectives, try_all_the_matrix(): all_to_all(jnp.stack(axis_size(row_axis) * [x_part]), row_axis, 0, 0)  20 us
    reduce_sum x1, other arithmetic, attend(): total = jnp.sum(expon, axis=2)  11.1 us
    unnamed x34, local copies, waits for them, and re-layouts  9.51 us
  transfers between devices with their start and end apart: 11, of which 6 were waited for; matrix products, arithmetic and copies ran while one was open for 36% of the time, Pallas kernels for 0%

profile of v1, /device:TPU:1, one launch (start us, length us, event | category | flops | bytes accessed | tf_op | source)
XLA Modules:
  0.0 301.9 jit_solution(13558590640570256749)
XLA Ops:
  7.3 2.1 copy.56
  9.4 2.4 reshape.105
  14.5 51.2 %all-gather.24.cloned.1.call-done = bf16[1794048]{0:T(1024)(128)(2,1)} async-done(((bf16[224256]{0:T(1024)(128)(2,1)}), bf16[1794048]{0:T(1024)(128)(2,1)}) %all-gather.24.cloned.1.call-update) | async-done | bytes 3588112 | tf_op jit(solution)/shard_map/all_gather | solution.py:99
  65.7 5.4 %reshape.120 = bf16[8,224256]{1,0:T(8,128)(2,1)} reshape(bf16[1794048]{0:T(1024)(128)(2,1)} %all-gather.24.cloned.1.call-done) | data formatting | bytes 7176192 | tf_op jit(solution)/shard_map/all_gather | solution.py:99
  73.6 2.8 reshape.130
  76.4 22.4 %reshape.108 = bf16[8,5,1408,24]{3,2,1,0:T(8,128)(2,1)} reshape(bf16[1351680]{0:T(1024)(128)(2,1)} %reshape.130) | data formatting | bytes 5406720 | tf_op jit(solution)/shard_map/reshape | solution.py:102
  98.8 10.0 %fusion.56 = (bf16[1,1408,8,24]{3,1,0,2:T(8,128)(2,1)S(1)}, bf16[1,1408,8,24]{3,1,0,2:T(8,128)(2,1)}, bf16[1,1408,8,24]{3,1,0,2:T(8,128)(2,1)}, bf16[1,1408,8,24]{3,1,0,2:T(8,128)(2,1)}, bf16[1,1408,8,24]{3,1,0,2:T(8,128)(2,1)}) fusion(bf16[5,1408,8,24]{3,1,0,2:T(8,128)(2,1)} %bitcast.79), kind=kLoop, calls=%fused_computation.61 | loop fusion | bytes 5406720 | tf_op jit(solution)/shard_map/slice | solution.py:31
  108.8 3.7 %copy.58 = bf16[1,1408,8,24]{1,3,2,0:T(8,128)(2,1)} copy(bf16[1,1408,8,24]{3,1,0,2:T(8,128)(2,1)} %get-tuple-element.13) | data formatting | bytes 1081344 | tf_op jit(solution)/shard_map/slice | solution.py:31
  112.5 3.8 %copy.59 = bf16[1,1408,8,24]{1,3,2,0:T(8,128)(2,1)} copy(bf16[1,1408,8,24]{3,1,0,2:T(8,128)(2,1)} %get-tuple-element.12) | data formatting | bytes 1081344 | tf_op jit(solution)/shard_map/slice | solution.py:31
  116.4 3.8 %copy.57 = bf16[1,1408,8,24]{1,3,2,0:T(8,128)(2,1)} copy(bf16[1,1408,8,24]{3,1,0,2:T(8,128)(2,1)} %get-tuple-element.14) | data formatting | bytes 1081344 | tf_op jit(solution)/shard_map/slice | solution.py:31
  120.2 3.8 %copy.61 = bf16[1,1408,8,24]{1,3,2,0:T(8,128)(2,1)} copy(bf16[1,1408,8,24]{3,1,0,2:T(8,128)(2,1)} %get-tuple-element.11) | data formatting | bytes 1081344 | tf_op jit(solution)/shard_map/slice | solution.py:31
  124.0 1.7 copy.60
  127.8 1.5 collective-permute-start.1
  129.3 6.1 %all-gather.12.cloned.1.call-done = bf16[768,1280]{1,0:T(8,128)(2,1)} async-done(((bf16[192,1280]{1,0:T(8,128)(2,1)}), bf16[768,1280]{1,0:T(8,128)(2,1)}) %all-gather.12.cloned.1.call-update) | async-done | bytes 1966096 | tf_op jit(solution)/shard_map/all_gather | solution.py:42
  135.4 2.7 constant_dynamic-update-slice_fusion.1
  139.1 1.6 fusion.58
  140.7 1.6 fusion.12
  142.3 1.6 fusion.8
  143.9 1.6 fusion.26
  145.6 1.7 fusion.20
  147.9 2.2 reduce_max.18
  151.6 4.2 %all-to-all-start = ((bf16[8,96,192]{1,2,0:T(8,128)(2,1)}), bf16[8,96,192]{1,2,0:T(8,128)(2,1)S(1)}, u32[]{:S(2)}, u32[]{:S(2)}) async-start(bf16[8,96,192]{1,2,0:T(8,128)(2,1)} %copy.64), calls=%async_computation | async-start | bytes 786432 | tf_op jit(solution)/shard_map/all_to_all | solution.py:127
  155.9 7.6 %all-to-all-done = bf16[8,96,192]{1,2,0:T(8,128)(2,1)S(1)} async-done(((bf16[8,96,192]{1,2,0:T(8,128)(2,1)}), bf16[8,96,192]{1,2,0:T(8,128)(2,1)S(1)}, u32[]{:S(2)}, u32[]{:S(2)}) %all-to-all-start) | async-done | bytes 294944 | tf_op jit(solution)/shard_map/all_to_all | solution.py:127
  164.1 2.8 convolution_convert_fusion.1
  166.9 20.0 %all_to_all.10 = bf16[8,96,256]{2,1,0:T(8,128)(2,1)} all-to-all(bf16[8,96,256]{2,1,0:T(8,128)(2,1)S(1)} %stack.2), channel_id=1, replica_groups=mesh['dp'=4,'sz'=8,'sxx'=4,'core'=2] {'sz'}, dimensions={0} | all-to-all | bytes 786432 | tf_op jit(solution)/shard_map/all_to_all | solution.py:14
  188.0 23.8 %all-gather.16.cloned.1.call-done = bf16[3072,256]{1,0:T(8,128)(2,1)} async-done(((bf16[768,256]{1,0:T(8,128)(2,1)}), bf16[3072,256]{1,0:T(8,128)(2,1)}) %all-gather.16.cloned.1.call-update) | async-done | bytes 1572880 | tf_op jit(solution)/shard_map/all_gather | solution.py:42
  213.1 29.5 %all-gather.20.cloned.1.call-done = bf16[512,1536]{1,0:T(8,128)(2,1)} async-done(((bf16[128,1536]{1,0:T(8,128)(2,1)}), bf16[512,1536]{1,0:T(8,128)(2,1)}) %all-gather.20.cloned.1.call-update) | async-done | bytes 1572880 | tf_op jit(solution)/shard_map/all_gather | solution.py:42
  242.5 20.2 %all-gather.18.cloned.1.call-done = bf16[6144,256]{1,0:T(8,128)(2,1)} async-done(((bf16[3072,256]{1,0:T(8,128)(2,1)}), bf16[6144,256]{1,0:T(8,128)(2,1)}) %all-gather.18.cloned.1.call-update) | async-done | bytes 3145744 | tf_op jit(solution)/shard_map/all_gather | solution.py:43
  262.7 9.2 %bitcast_reduce_fusion = (f32[8,96]{1,0:T(8,128)S(1)}, f32[6144,96,8]{0,1,2:T(8,128)}) fusion(f32[8]{0:T(128)S(1)} %copy-done.8, bf16[6144,256]{1,0:T(8,128)(2,1)} %all-gather.18.cloned.1.call-done, bf16[96,1280]{1,0:T(8,128)(2,1)S(1)} %convolution_convert_fusion.1), kind=kOutput, calls=%fused_computation.1 | convolution fusion | flops 1222114560 | bytes 20647424 | tf_op jit(solution)/shard_map/qhd,kd->hqk/dot_general | solution.py:62
  271.9 11.1 %fusion.1 = f32[8,96]{1,0:T(8,128)S(1)} fusion(f32[6144,96,8]{0,1,2:T(8,128)} %get-tuple-element.18, f32[8,96]{1,0:T(8,128)S(1)} %get-tuple-element.17, f32[8]{0:T(128)S(1)} %copy-done.8), kind=kLoop, calls=%fused_computation.4 | loop fusion | flops 18873600 | bytes 18880544 | tf_op jit(solution)/shard_map/reduce_sum | solution.py:68
  283.1 8.4 %fusion.46 = bf16[96,8,128]{2,0,1:T(8,128)(2,1)S(1)} fusion(bf16[6144,256]{1,0:T(8,128)(2,1)S(1)} %copy-done.1, f32[6144,96,8]{0,1,2:T(8,128)} %get-tuple-element.18, f32[8,96]{1,0:T(8,128)S(1)} %get-tuple-element.17, f32[8]{0:T(128)S(1)} %copy-done.8, f32[96,8]{0,1:T(8,128)S(1)} %bitcast.95), kind=kOutput, calls=%fused_computation.43 | convolution fusion | flops 1227030528 | bytes 20652544 | tf_op jit(solution)/shard_map/hqk,kd->hqd/dot_general | solution.py:69
  291.8 3.3 %convolution_convert_fusion = bf16[96,1536]{1,0:T(8,128)(2,1)} fusion(bf16[96,1024]{0,1:T(8,128)(2,1)S(1)} %bitcast.88, bf16[1024,1536]{1,0:T(8,128)(2,1)} %all-gather.22.cloned.1.call-done), kind=kOutput, calls=%fused_computation.23 | convolution fusion | flops 302137344 | bytes 3637248 | tf_op jit(solution)/shard_map/dot_general | solution.py:143
  (88 shorter events, 13.5 us)
Async XLA Ops:
  7.2 4.6 %copy-start.7 = (bf16[24,1024]{1,0:T(8,128)(2,1)S(1)}, bf16[24,1024]{1,0:T(8,128)(2,1)}, u32[]{:S(2)}) copy-start(bf16[24,1024]{1,0:T(8,128)(2,1)} %param.14) | copy-start | bytes 147460
  7.2 4.6 %copy-start.9 = (bf16[24,256]{1,0:T(8,128)(2,1)S(1)}, bf16[24,256]{1,0:T(8,128)(2,1)}, u32[]{:S(2)}) copy-start(bf16[24,256]{1,0:T(8,128)(2,1)} %param.15) | copy-start | bytes 36868
  7.2 4.8 %copy-start.6 = (bf16[16,1536]{1,0:T(8,128)(2,1)S(1)}, bf16[16,1536]{1,0:T(8,128)(2,1)}, u32[]{:S(2)}) copy-start(bf16[16,1536]{1,0:T(8,128)(2,1)} %param.17) | copy-start | bytes 147460
  7.2 5.7 %copy-start = (bf16[192,1408]{1,0:T(8,128)(2,1)S(1)}, bf16[192,1408]{1,0:T(8,128)(2,1)}, u32[]{:S(2)}) copy-start(bf16[192,1408]{1,0:T(8,128)(2,1)} %param.9) | copy-start | bytes 1622020
  7.2 5.9 %copy-start.10 = (f32[1408]{0:T(1024)S(1)}, f32[1408]{0:T(1024)}, u32[]{:S(2)}) copy-start(f32[1408]{0:T(1024)} %param.10) | copy-start | bytes 16900
  7.2 58.5 %all-gather.24.cloned.1.call-start = ((), (), s32[]{:S(2)}) async-start(), calls=%async_computation.9 | async-start | bytes 4036608 | tf_op jit(solution)/shard_map/all_gather | solution.py:99
  12.9 112.8 %all-gather.10.cloned.1.call-start = ((), (), s32[]{:S(2)}) async-start(), calls=%async_computation.2 | async-start | bytes 4866048 | tf_op jit(solution)/shard_map/all_gather | solution.py:113
  14.5 59.0 %copy-start.11 = (f32[1536]{0:T(1024)S(1)}, f32[1536]{0:T(1024)}, u32[]{:S(2)}) copy-start(f32[1536]{0:T(1024)} %param.12) | copy-start | bytes 18436
  14.5 120.9 %all-gather.12.cloned.1.call-start = ((), (), s32[]{:S(2)}) async-start(), calls=%async_computation.3 | async-start | bytes 2457600 | tf_op jit(solution)/shard_map/all_gather | solution.py:42
  71.1 2.6 slice-start
  73.4 90.7 %all-gather.14.cloned.1.call-start = ((), (), s32[]{:S(2)}) async-start(), calls=%async_computation.4 | async-start | bytes 5898240 | tf_op jit(solution)/shard_map/all_gather | solution.py:43
  126.5 14.2 %collective-permute-start = (bf16[2,1408]{1,0:T(2,128)(2,1)S(1)}, bf16[2,1408]{1,0:T(2,128)(2,1)S(1)}, u32[]{:S(2)}, u32[]{:S(2)}) collective-permute-start(bf16[2,1408]{1,0:T(2,128)(2,1)S(1)} %get-tuple-element.15), channel_id=1, source_target_pairs={{0,8},{8,16},{16,24},{24,32},{32,40},{40,48},{48,56},{1,9},{9,17},... | collective-permute-start | bytes 16904 | tf_op jit(solution)/shard_map/ppermute | solution.py:117
  127.8 12.8 %collective-permute-start.1 = (bf16[2,1408]{1,0:T(2,128)(2,1)S(1)}, bf16[2,1408]{1,0:T(2,128)(2,1)S(1)}, u32[]{:S(2)}, u32[]{:S(2)}) collective-permute-start(bf16[2,1408]{1,0:T(2,128)(2,1)S(1)} %get-tuple-element.16), channel_id=1, source_target_pairs={{8,0},{16,8},{24,16},{32,24},{40,32},{48,40},{56,48},{9,1},{17,9},... | collective-permute-start | bytes 16904 | tf_op jit(solution)/shard_map/ppermute | solution.py:118
  135.4 2.8 slice-start.2
  135.4 3.5 %slice-start.3 = ((s8[4325376]{0:T(1024)(128)(4,1)}), s8[4194304]{0:T(1024)(128)(4,1)S(1)}, s32[]{:S(2)}) async-start(s8[4325376]{0:T(1024)(128)(4,1)} %bitcast.83), calls=%async_computation.13 | async-start | bytes 8388608
  135.4 3.6 %copy-start.5 = (bf16[1,1408,8,24]{1,3,2,0:T(8,128)(2,1)S(1)}, bf16[1,1408,8,24]{1,3,2,0:T(8,128)(2,1)}, u32[]{:S(2)}) copy-start(bf16[1,1408,8,24]{1,3,2,0:T(8,128)(2,1)} %copy.59) | copy-start | bytes 1622020
  138.1 2.6 copy-start.3
  140.7 1.6 copy-start.4
  142.3 1.6 copy-start.2
  147.3 8.5 %copy-start.12 = (f32[1536]{0:T(1024)S(1)}, f32[1536]{0:T(1024)}, u32[]{:S(2)}) copy-start(f32[1536]{0:T(1024)} %param.13) | copy-start | bytes 18436
  151.6 11.9 %all-to-all-start = ((bf16[8,96,192]{1,2,0:T(8,128)(2,1)}), bf16[8,96,192]{1,2,0:T(8,128)(2,1)S(1)}, u32[]{:S(2)}, u32[]{:S(2)}) async-start(bf16[8,96,192]{1,2,0:T(8,128)(2,1)} %copy.64), calls=%async_computation | async-start | bytes 786432 | tf_op jit(solution)/shard_map/all_to_all | solution.py:127
  155.8 56.0 %all-gather.16.cloned.1.call-start = ((), (), s32[]{:S(2)}) async-start(), calls=%async_computation.5 | async-start | bytes 1966080 | tf_op jit(solution)/shard_map/all_gather | solution.py:42
  163.7 23.2 %slice-start.1 = ((bf16[8,224256]{1,0:T(8,128)(2,1)}), bf16[8,24576]{1,0:T(8,128)(2,1)S(1)}, s32[]{:S(2)}) async-start(bf16[8,224256]{1,0:T(8,128)(2,1)} %reshape.120), calls=%async_computation.11 | async-start | bytes 786432 | tf_op jit(solution)/shard_map/slice | solution.py:109
  166.9 95.8 %copy-start.8 = (f32[8]{0:T(128)S(1)}, f32[8]{0:T(128)}, u32[]{:S(2)}) copy-start(f32[8]{0:T(128)} %param.16) | copy-start | bytes 100
  186.9 55.6 %all-gather.20.cloned.1.call-start = ((), (), s32[]{:S(2)}) async-start(), calls=%async_computation.7 | async-start | bytes 1966080 | tf_op jit(solution)/shard_map/all_gather | solution.py:42
  188.0 74.8 %all-gather.18.cloned.1.call-start = ((), (), s32[]{:S(2)}) async-start(), calls=%async_computation.6 | async-start | bytes 4718592 | tf_op jit(solution)/shard_map/all_gather | solution.py:43
  211.9 79.9 %all-gather.22.cloned.1.call-start = ((), (), s32[]{:S(2)}) async-start(), calls=%async_computation.8 | async-start | bytes 4718592 | tf_op jit(solution)/shard_map/all_gather | solution.py:43
  271.9 11.1 %copy-start.1 = (bf16[6144,256]{1,0:T(8,128)(2,1)S(1)}, bf16[6144,256]{1,0:T(8,128)(2,1)}, u32[]{:S(2)}) copy-start(bf16[6144,256]{1,0:T(8,128)(2,1)} %all-gather.18.cloned.1.call-done) | copy-start | bytes 9437188
Sparse Core Ops, SparseCore 0:
  13.0 52.6 all-gather.23
  67.6 34.2 all-gather.9
  103.7 31.6 all-gather.11
  137.0 19.5 all-gather.13
  187.1 24.7 all-gather.15
  213.5 28.9 all-gather.19
  244.3 18.3 all-gather.17
  264.5 18.7 all-gather.21
